TPU v7x, 128 devices: a whole 4x4x4 slice. The times are simulated.
128 devices in a mesh: seq: 16 (over x_hi, y, core), head: 8 (over x_lo, z).
Axes of the slice: x: 4 (x_hi: 2, x_lo: 2; x = x_hi * 2 + x_lo), y: 4, z: 4, core: 2. Of those that a mesh axis runs over, the one named last changes fastest.
Arguments:
- tokens: bfloat16 [4096, 2048], P('seq'), may hold values from -6 to 6
- norm_gain: float32 [2048], replicated, may hold values from 0.1 to 1.9
- w_query: bfloat16 [2048, 4096], P(None, 'head')
- w_key: bfloat16 [2048, 512], replicated
- w_value: bfloat16 [2048, 512], replicated, may hold values from -0.125 to 0.125
- query_gain: float32 [128], replicated, may hold values from 0.5 to 5.5
- key_gain: float32 [128], replicated, may hold values from 0.5 to 5.5
- w_out: bfloat16 [4096, 2048], P('head'), may hold values from -0.5 to 0.5
- post_gain: float32 [2048], replicated, may hold values from 0.1 to 1.9
- doc_lengths: int32 [6], replicated, may hold values from 1 to 2560, 4096 in all
- expert_ids: int32 [4096, 8], P(('seq', 'head')), may hold values from 0 to 127, all different within a row; in each aligned block of 32 rows (0 to 31, 32 to 63, ...) at most 4 rows name the same one
- route_weights: float32 [4096, 8], P(('seq', 'head')), may hold values from 0.15 to 1
- w_gate: bfloat16 [128, 2048, 768], P(('seq', 'head')), may hold values from -0.125 to 0.125
- w_up: bfloat16 [128, 2048, 768], P(('seq', 'head')), may hold values from -0.125 to 0.125
- w_down: bfloat16 [128, 768, 2048], P(('seq', 'head')), may hold values from -0.21875 to 0.21875
Outputs:
- layer_out: bfloat16 [4096, 2048], P(('seq', 'head'))
Inputs may be any that keep to these rules, and one draw needn't show every extreme that they name: `doc_lengths`: 6 document lengths that sum to 4096; the largest is exactly 2560. `expert_ids`: each row names 8 different experts. Among the 32 rows of one device no expert is named more than 4 times; in some devices' rows some expert is named exactly 4 times.
All inputs are finite; a program needn't handle non-finite values.
Results may differ from a plain program's by a relative error of at most 0.015.
The roundings to bfloat16 on the way count: a program that leaves them out, or rounds other values in their place, can miss the bound.
Values may be sent and summed in bfloat16 or wider, within the bound.
No kernel may reach another device: no remote copies, remote signals or barrier semaphores. Data moves between devices by JAX's collectives and lax.ppermute only.
A program may use at most 128 MiB of HBM per device.

v0:
```python
import math
import jax
import jax.numpy as jnp
from jax import lax
from jax.sharding import PartitionSpec as P

HEADS = 32
KV_HEADS = 4
TOP = 8
EPSILON = 1e-06
THETA = 1000000.0
FLOOR = -1e30


def rms_scale(values, gain):
    return values * lax.rsqrt(jnp.mean(values * values, axis=-1, keepdims=True) + EPSILON) * gain


def rotate(values, cosine, sine):
    half = values.shape[-1] // 2
    first = values[..., :half]
    second = values[..., half:]
    return jnp.concatenate(
        [first * cosine - second * sine, second * cosine + first * sine], axis=-1
    )


def doc_index(positions, ends):
    return jnp.sum((positions[:, None] >= ends[None, :]).astype(jnp.int32), axis=1)


def local(
    tokens,
    norm_gain,
    w_query,
    w_key,
    w_value,
    query_gain,
    key_gain,
    w_out,
    post_gain,
    doc_lengths,
    expert_ids,
    route_weights,
    w_gate,
    w_up,
    w_down,
):
    tok_dev, width = tokens.shape
    head_dim = query_gain.shape[0]
    per_dev = w_query.shape[1] // head_dim
    n_seq = lax.axis_size("seq")
    n_head = lax.axis_size("head")
    seq_index = lax.axis_index("seq")
    head_index = lax.axis_index("head")
    ndocs = doc_lengths.shape[0]
    ends = jnp.cumsum(doc_lengths)
    starts = ends - doc_lengths
    positions = seq_index * tok_dev + jnp.arange(tok_dev, dtype=jnp.int32)
    query_doc = doc_index(positions, ends)
    matches = query_doc[:, None] == jnp.arange(ndocs, dtype=jnp.int32)[None, :]
    own_start = jnp.sum(jnp.where(matches, starts[None, :], 0), axis=1)
    offset = (positions - own_start).astype(jnp.float32)
    half = head_dim // 2
    inverse = THETA ** (-2.0 * jnp.arange(half, dtype=jnp.float32) / head_dim)
    angles = offset[:, None] * inverse[None, :]
    cosine = jnp.cos(angles)
    sine = jnp.sin(angles)
    inputs = tokens.astype(jnp.float32)
    normed = rms_scale(inputs, norm_gain).astype(jnp.bfloat16)
    queries = jnp.dot(normed, w_query, preferred_element_type=jnp.float32).reshape(
        tok_dev, per_dev, head_dim
    )
    queries = rotate(rms_scale(queries, query_gain), cosine[:, None, :], sine[:, None, :]).astype(
        jnp.bfloat16
    )
    column = head_index * per_dev // (HEADS // KV_HEADS) * head_dim
    key_cols = lax.dynamic_slice_in_dim(w_key, column, head_dim, 1)
    value_cols = lax.dynamic_slice_in_dim(w_value, column, head_dim, 1)
    keys = rotate(
        rms_scale(jnp.dot(normed, key_cols, preferred_element_type=jnp.float32), key_gain),
        cosine,
        sine,
    ).astype(jnp.bfloat16)
    values = jnp.dot(normed, value_cols, preferred_element_type=jnp.float32).astype(jnp.bfloat16)
    stacked = jnp.stack([keys, values])
    scale = head_dim ** (-0.5)
    last_query = positions[-1]
    first_start = own_start[0]

    def attend(state, block, key_start):
        count = block.shape[1]
        key_pos = key_start + jnp.arange(count, dtype=jnp.int32)

        def update(carry):
            high, total, accum = carry
            key_doc = doc_index(key_pos, ends)
            allowed = (
                (key_doc[None, :] == query_doc[:, None])
                & (key_pos[None, :] <= positions[:, None])
                & (key_pos[None, :] >= 0)
            )
            scores = (
                jnp.einsum("qhd,kd->hqk", queries, block[0], preferred_element_type=jnp.float32)
                * scale
            )
            scores = jnp.where(allowed[None], scores, FLOOR)
            new_high = jnp.maximum(high, jnp.max(scores, axis=2))
            weights = jnp.where(allowed[None], jnp.exp(scores - new_high[:, :, None]), 0.0)
            factor = jnp.exp(high - new_high)
            total = total * factor + jnp.sum(weights, axis=2)
            accum = accum * jnp.transpose(factor)[:, :, None] + jnp.einsum(
                "hqk,kd->qhd",
                weights.astype(jnp.bfloat16),
                block[1],
                preferred_element_type=jnp.float32,
            )
            return (new_high, total, accum)

        needed = (key_start <= last_query) & (key_start + count - 1 >= first_start)
        return lax.cond(needed, update, lambda carry: carry, state)

    initial = (
        jnp.full((per_dev, tok_dev), FLOOR, jnp.float32),
        jnp.zeros((per_dev, tok_dev), jnp.float32),
        jnp.zeros((tok_dev, per_dev, head_dim), jnp.float32),
    )
    piece = lax.all_gather(stacked, "seq", axis=1, tiled=True)
    count = piece.shape[1]
    step = math.gcd(count, tok_dev * max(1, 512 // tok_dev))

    def inner(index, carry):
        block = lax.dynamic_slice_in_dim(piece, index * step, step, 1)
        return attend(carry, block, index * step)

    state = lax.fori_loop(0, count // step, inner, initial)
    high, total, accum = state
    attended = (
        (accum / jnp.transpose(total)[:, :, None])
        .astype(jnp.bfloat16)
        .reshape(tok_dev, per_dev * head_dim)
    )
    rows = tok_dev // n_head
    attn_rows = lax.psum_scatter(
        jnp.dot(attended, w_out, preferred_element_type=jnp.float32).astype(jnp.bfloat16),
        "head",
        scatter_dimension=0,
        tiled=True,
    ).astype(jnp.float32)
    resid = lax.dynamic_slice_in_dim(inputs, head_index * rows, rows, 0) + attn_rows
    routed = rms_scale(resid, post_gain).astype(jnp.bfloat16)
    experts = n_seq * n_head * w_gate.shape[0]
    capacity = 2 * TOP * rows // experts
    chosen = expert_ids.reshape(-1)
    hits = (chosen[:, None] == jnp.arange(experts, dtype=jnp.int32)[None, :]).astype(jnp.int32)
    rank = jnp.sum((jnp.cumsum(hits, axis=0) - hits) * hits, axis=1)
    target = chosen * capacity + rank
    outgoing = (
        jnp.zeros((experts * capacity, width), jnp.bfloat16)
        .at[target]
        .set(jnp.repeat(routed, TOP, axis=0))
    )
    outgoing = outgoing.reshape(experts, capacity, width)
    block = lax.all_to_all(outgoing, ("seq", "head"), split_axis=0, concat_axis=0, tiled=True)
    flat = block.reshape(-1, width)
    gate = jnp.dot(flat, w_gate[0], preferred_element_type=jnp.float32)
    up = jnp.dot(flat, w_up[0], preferred_element_type=jnp.float32)
    hidden = (jax.nn.silu(gate) * up).astype(jnp.bfloat16)
    returned = lax.all_to_all(
        jnp.dot(hidden, w_down[0], preferred_element_type=jnp.float32)
        .astype(jnp.bfloat16)
        .reshape(block.shape),
        ("seq", "head"),
        split_axis=0,
        concat_axis=0,
        tiled=True,
    )
    picked = returned.reshape(experts * capacity, width)[target].reshape(rows, TOP, width)
    combined = jnp.sum(picked.astype(jnp.float32) * route_weights[:, :, None], axis=1)
    return (resid + combined).astype(jnp.bfloat16)


def solution(mesh):
    placed = (
        P("seq", None),
        P(),
        P(None, "head"),
        P(),
        P(),
        P(),
        P(),
        P("head", None),
        P(),
        P(),
        P(("seq", "head"), None),
        P(("seq", "head"), None),
        P(("seq", "head"), None, None),
        P(("seq", "head"), None, None),
        P(("seq", "head"), None, None),
    )
    return jax.shard_map(
        local, mesh=mesh, in_specs=placed, out_specs=P(("seq", "head"), None), check_vma=False
    )
```

profile of v0, /device:TPU:0, one launch (start us, length us, event | category | flops | bytes accessed | tf_op | source)
XLA Modules:
  0.0 291.0 jit_solution(13176573164525477628)
XLA Ops:
  17.5 3.5 %fusion.51 = f32[256,512]{1,0:T(8,128)} fusion(bf16[2048,512]{1,0:T(8,128)(2,1)} %param.21, f32[2048]{0:T(1024)S(1)} %copy-done.9, f32[256]{0:T(256)S(1)} %add_rsqrt_fusion.2, bf16[256,2048]{1,0:T(8,128)(2,1)} %param.19), kind=kOutput, calls=%fused_computation.99 | convolution fusion | flops 538968064 | bytes 3679232 | tf_op jit(solution)/shard_map/dot_general | solution.py:71
  20.9 2.0 reshape.304
  26.1 39.4 %all-gather.2.cloned.1.call-done = bf16[2,4096,128]{1,2,0:T(8,128)(2,1)} async-done(((bf16[2,256,128]{1,2,0:T(8,128)(2,1)}), bf16[2,4096,128]{1,2,0:T(8,128)(2,1)}) %all-gather.2.cloned.1.call-update) | async-done | bytes 2097168 | tf_op jit(solution)/shard_map/all_gather | solution.py:128
  65.6 4.1 %copy.70 = bf16[2,4096,128]{2,1,0:T(8,128)(2,1)} copy(bf16[2,4096,128]{1,2,0:T(8,128)(2,1)} %all-gather.2.cloned.1.call-done) | data formatting | bytes 4194304
  70.5 18.4 %while.22 = (s32[]{:T(128)}, f32[4,256]{1,0:T(4,128)S(1)}, f32[4,256]{1,0:T(4,128)S(1)}, f32[256,4,128]{2,0,1:T(8,128)}, s32[]{:T(128)}, /*index=5*/s32[]{:T(128...) while((s32[]{:T(128)}, f32[4,256]{1,0:T(4,128)S(1)}, ...), condition=%wide.region_12.13_spmd.clone, body=%wide.region_6.12_spmd.clone.sunk | while | flops 276050688 | bytes 16863676 | solution.py:136
  71.7 8.4 %conditional.3 = ((f32[4,256]{1,0:T(4,128)S(1)}, f32[4,256]{1,0:T(4,128)S(1)}, f32[256,4,128]{2,0,1:T(8,128)})) conditional(s32[]{:T(128)} %convert_element_type.143, (f32[4,256]{1,0:T(4,128)S(1)}, f32[4,256]{1,0:T(4,128)S(1)}, f32[256,4,128]{2,0,1:T(8,128)}) %tuple.83, (s32[]{:T(128)}, s32[512]{0:T(512)S(1)}, s32[6]{0:T(128)}, s32[256]{0:T(256)}, ...), branch_computations={%region_7.7_spmd, %region_8.11_spmd} | conditional | flops 276050688 | bytes 16860310 | solution.py:121
  73.4 2.7 fusion.2
  76.1 3.5 %fusion.5 = f32[256,4,128]{2,0,1:T(8,128)} fusion(f32[512,256,4]{1,0,2:T(8,128)} %get-tuple-element.592, f32[4,256]{1,0:T(4,128)S(1)} %get-tuple-element.679, pred[256,512]{0,1:T(8,128)(4,1)S(1)} %and_and_fusion, f32[256,4,128]{2,0,1:T(8,128)} %get-tuple-element.459, f32[256,4]{0,1:T(4,128)S(1)} %get-tuple-element.587, ...), kind=kOutput, calls=%fused_computation.9 | convolution fusion | flops 137101312 | bytes 3416072 | tf_op jit(solution)/shard_map/while/body/eval_jaxpr/cond/branch_1_fun/hqk,kd->qhd/dot_general | solution.py:112
  88.9 2.0 copy.71
  92.1 3.3 %convolution_convert_fusion = bf16[256,2048]{1,0:T(8,128)(2,1)} fusion(bf16[256,512]{0,1:T(8,128)(2,1)S(1)} %bitcast.89, bf16[512,2048]{1,0:T(8,128)(2,1)} %param.26), kind=kOutput, calls=%fused_computation.37 | convolution fusion | flops 537395200 | bytes 3407872 | tf_op jit(solution)/shard_map/dot_general | solution.py:145
  95.4 2.8 convert_element_type.85
  99.3 66.3 %reduce-scatter.2.cloned.1.call-done = bf16[32,2048]{1,0:T(8,128)(2,1)} async-done(((bf16[256,2048]{1,0:T(8,128)(2,1)}), bf16[32,2048]{1,0:T(8,128)(2,1)}) %reduce-scatter.2.cloned.1.call-update) | async-done | bytes 131088 | tf_op jit(solution)/shard_map/reduce_scatter | solution.py:144
  167.9 3.7 %scatter_custom_fusion = bf16[512,2048]{1,0:T(8,128)(2,1)} fusion(s32[256]{0:T(256)S(1)} %bitcast.95, bf16[]{:T(256)} %constant.154.clone.1, bf16[32,2048]{1,0:T(8,128)(2,1)S(1)} %multiply_convert_fusion.2), kind=kCustom, calls=%fused_computation.45 | custom fusion | bytes 2228226 | tf_op jit(solution)/shard_map/scatter | solution.py:161
  171.6 4.1 %reshape.308 = bf16[128,4,2048]{2,1,0:T(4,128)(2,1)} reshape(bf16[512,2048]{1,0:T(8,128)(2,1)} %scatter_custom_fusion) | data formatting | bytes 4194304 | tf_op jit(solution)/shard_map/reshape | solution.py:163
  175.7 37.7 %all_to_all.10 = bf16[128,4,2048]{2,1,0:T(4,128)(2,1)} all-to-all(bf16[128,4,2048]{2,1,0:T(4,128)(2,1)} %reshape.308), channel_id=1, replica_groups=mesh['seq'=16,'head'=8] {'seq','head'}, dimensions={0} | all-to-all | bytes 4194304 | tf_op jit(solution)/shard_map/all_to_all | solution.py:164
  213.5 4.0 %reshape.309 = bf16[512,2048]{1,0:T(8,128)(2,1)} reshape(bf16[128,4,2048]{2,1,0:T(4,128)(2,1)} %all_to_all.10) | data formatting | bytes 4194304 | tf_op jit(solution)/shard_map/reshape | solution.py:165
  217.4 5.5 %fusion.22 = f32[512,768]{1,0:T(8,128)} fusion(bf16[512,2048]{1,0:T(8,128)(2,1)} %reshape.309, bf16[1,2048,768]{2,1,0:T(8,128)(2,1)} %param.31), kind=kOutput, calls=%fused_computation.34 | convolution fusion | flops 1610612736 | bytes 6815744 | tf_op jit(solution)/shard_map/dot_general | solution.py:166
  222.9 8.3 %fusion.24 = bf16[512,2048]{1,0:T(8,128)(2,1)} fusion(bf16[1,768,2048]{2,1,0:T(8,128)(2,1)S(1)} %copy-done, f32[512,768]{1,0:T(8,128)} %fusion.22, bf16[512,2048]{1,0:T(8,128)(2,1)} %reshape.309, bf16[1,2048,768]{2,1,0:T(8,128)(2,1)} %param.32), kind=kOutput, calls=%fused_computation.36 | convolution fusion | flops 3224633344 | bytes 12058624 | tf_op jit(solution)/shard_map/dot_general | solution.py:170
  231.2 4.1 %reshape.310 = bf16[128,4,2048]{2,1,0:T(4,128)(2,1)} reshape(bf16[512,2048]{1,0:T(8,128)(2,1)} %fusion.24) | data formatting | bytes 4194304 | tf_op jit(solution)/shard_map/reshape | solution.py:172
  235.3 5.9 %all-to-all-start.1 = ((bf16[128,4,2048]{2,1,0:T(4,128)(2,1)}), bf16[128,4,2048]{2,1,0:T(4,128)(2,1)}, u32[]{:S(2)}, u32[]{:S(2)}) async-start(bf16[128,4,2048]{2,1,0:T(4,128)(2,1)} %reshape.310), calls=%async_computation.2 | async-start | bytes 4194304 | tf_op jit(solution)/shard_map/all_to_all | solution.py:169
  241.3 29.7 %all-to-all-done.1 = bf16[128,4,2048]{2,1,0:T(4,128)(2,1)} async-done(((bf16[128,4,2048]{2,1,0:T(4,128)(2,1)}), bf16[128,4,2048]{2,1,0:T(4,128)(2,1)}, u32[]{:S(2)}, u32[]{:S(2)}) %all-to-all-start.1) | async-done | bytes 2097184 | tf_op jit(solution)/shard_map/all_to_all | solution.py:169
  271.0 4.0 %reshape.311 = bf16[512,2048]{1,0:T(8,128)(2,1)} reshape(bf16[128,4,2048]{2,1,0:T(4,128)(2,1)} %all-to-all-done.1) | data formatting | bytes 4194304 | tf_op jit(solution)/shard_map/reshape | solution.py:178
  275.0 5.2 %gather_fusion = bf16[256,2048]{1,0:T(8,128)(2,1)} fusion(bf16[512,2048]{1,0:T(8,128)(2,1)} %reshape.311, s32[1024]{0:T(1024)S(1)} %pad_clamp_fusion), kind=kCustom, calls=%fused_computation | custom fusion | bytes 2098176 | tf_op jit(solution)/shard_map/gather | solution.py:178
  280.2 2.2 fusion.27
  (108 shorter events, 23.3 us)
Async XLA Ops:
  6.5 216.4 %copy-start = (bf16[1,768,2048]{2,1,0:T(8,128)(2,1)S(1)}, bf16[1,768,2048]{2,1,0:T(8,128)(2,1)}, u32[]{:S(2)}) copy-start(bf16[1,768,2048]{2,1,0:T(8,128)(2,1)} %param.33) | copy-start | bytes 9437188
  6.5 6.5 %copy-start.9 = (f32[2048]{0:T(1024)S(1)}, f32[2048]{0:T(1024)}, u32[]{:S(2)}) copy-start(f32[2048]{0:T(1024)} %param.20) | copy-start | bytes 24580
  6.5 3.7 %copy-start.10 = (s32[6]{0:T(128)S(1)}, s32[6]{0:T(128)}, u32[]{:S(2)}) copy-start(s32[6]{0:T(128)} %param.28) | copy-start | bytes 76
  6.5 59.0 %all-gather.2.cloned.1.call-start = ((), (), s32[]{:S(2)}) async-start(), calls=%async_computation.3 | async-start | bytes 2228224 | tf_op jit(solution)/shard_map/all_gather | solution.py:128
  8.3 6.7 %copy-start.7 = (f32[128]{0:T(128)S(1)}, f32[128]{0:T(128)}, u32[]{:S(2)}) copy-start(f32[128]{0:T(128)} %param.25) | copy-start | bytes 1540
  12.4 0.6 copy-start.3
  16.1 149.5 %reduce-scatter.2.cloned.1.call-start = ((), (), s32[]{:S(2)}) async-start(), calls=%async_computation.4 | async-start | bytes 1179648 | tf_op jit(solution)/shard_map/reduce_scatter | solution.py:144
  17.4 7.0 %copy-start.8 = (f32[128]{0:T(128)S(1)}, f32[128]{0:T(128)}, u32[]{:S(2)}) copy-start(f32[128]{0:T(128)} %param.24) | copy-start | bytes 1540
  76.1 3.5 %copy-start.1 = (f32[512,256,4]{1,0,2:T(8,128)S(1)}, f32[512,256,4]{1,0,2:T(8,128)}, u32[]{:S(2)}) copy-start(f32[512,256,4]{1,0,2:T(8,128)} %get-tuple-element.592) | copy-start | bytes 6291460 | tf_op jit(solution)/shard_map/while/body/eval_jaxpr/cond
  95.4 2.9 copy-start.4
  95.4 71.4 %copy-start.5 = (f32[2048]{0:T(1024)S(1)}, f32[2048]{0:T(1024)}, u32[]{:S(2)}) copy-start(f32[2048]{0:T(1024)} %param.27) | copy-start | bytes 24580
  235.3 5.9 %copy-start.6 = (f32[32,8]{0,1:T(8,128)S(1)}, f32[32,8]{0,1:T(8,128)}, u32[]{:S(2)}) copy-start(f32[32,8]{0,1:T(8,128)} %param.30) | copy-start | bytes 3076
  235.3 35.7 %all-to-all-start.1 = ((bf16[128,4,2048]{2,1,0:T(4,128)(2,1)}), bf16[128,4,2048]{2,1,0:T(4,128)(2,1)}, u32[]{:S(2)}, u32[]{:S(2)}) async-start(bf16[128,4,2048]{2,1,0:T(4,128)(2,1)} %reshape.310), calls=%async_computation.2 | async-start | bytes 4194304 | tf_op jit(solution)/shard_map/all_to_all | solution.py:169
  275.0 7.5 %copy-start.2 = (bf16[32,2048]{1,0:T(8,128)(2,1)S(1)}, bf16[32,2048]{1,0:T(8,128)(2,1)}, u32[]{:S(2)}) copy-start(bf16[32,2048]{1,0:T(8,128)(2,1)} %reduce-scatter.2.cloned.1.call-done) | copy-start | bytes 393220
Sparse Core Ops, SparseCore 0:
  16.2 49.3 all-gather.1
  95.5 70.0 reduce-scatter.1
where the time goes:
time: 292 us; the launch traced here: 291 us
  waiting for transfers between devices  135 us (46%)
  blocking collectives  37.7 us (13%)
  local copies, waits for them, and re-layouts  36.7 us (13%)
  matrix products  30.5 us (10%)
  other arithmetic  20.8 us (7%)
  between operations  13.7 us (5%)
  loops' own time  10 us (3%)
  starting transfers between devices  5.95 us (2%)
    reduce_scatter x1, waiting for transfers between devices, local(): lax.psum_scatter(jnp.dot(attended, w_out, preferred_element_type=jnp.floa...  66.3 us
    all_gather x1, waiting for transfers between devices, local(): piece = lax.all_gather(stacked, 'seq', axis=1, tiled=True)  39.4 us
    all_to_all x1, blocking collectives, local(): lax.all_to_all(outgoing, ('seq', 'head'), split_axis=0, concat_axis=0, ti...  37.7 us
    all_to_all x1, waiting for transfers between devices, local(): lax.all_to_all(jnp.dot(hidden, w_down[0], preferred_element_type=jnp.floa...  29.7 us
    another operation x1, loops' own time, local(): state = lax.fori_loop(0, count // step, inner, initial)  9.87 us
    dot_general x1, matrix products, local(): jnp.dot(hidden, w_down[0], preferred_element_type=jnp.float32)  8.26 us
    all_to_all x1, starting transfers between devices, local(): lax.all_to_all(jnp.dot(hidden, w_down[0], preferred_element_type=jnp.floa...  5.91 us
  transfers between devices with their start and end apart: 3, of which 3 were waited for; matrix products, arithmetic and copies ran while one was open for 5% of the time, Pallas kernels for 0%

commit v1 on v0

--- a/solution.py
+++ b/solution.py
@@ -125,7 +125,9 @@
         jnp.zeros((per_dev, tok_dev), jnp.float32),
         jnp.zeros((tok_dev, per_dev, head_dim), jnp.float32),
     )
-    piece = lax.all_gather(stacked, "seq", axis=1, tiled=True)
+    piece = jnp.concatenate(
+        lax.all_to_all(jnp.stack([stacked] * lax.axis_size("seq")), "seq", 0, 0), axis=1
+    )
     count = piece.shape[1]
     step = math.gcd(count, tok_dev * max(1, 512 // tok_dev))
 

time: 292 us -> 281 us (0.962)
  waiting for transfers between devices: 135 us -> 116 us
  starting transfers between devices: 5.95 us -> 13.1 us
    all_gather x1 -> x0, waiting for transfers between devices: 39.4 us -> none  [local(): piece = lax.all_gather(stacked, 'seq', axis=1, tiled=True)]
    all_to_all x0 -> x1, waiting for transfers between devices: none -> 19.2 us  [local(): lax.all_to_all(jnp.stack([stacked] * lax.axis_size('seq')), 'seq', 0, 0)]
    all_to_all x0 -> x1, starting transfers between devices: none -> 7.16 us  [local(): lax.all_to_all(jnp.stack([stacked] * lax.axis_size('seq')), 'seq', 0, 0)]
    unnamed x24 -> x23, local copies, waits for them, and re-layouts: 4.77 us -> 0.67 us
    all_to_all x0 -> x1, local copies, waits for them, and re-layouts: none -> 3.17 us  [local(): lax.all_to_all(jnp.stack([stacked] * lax.axis_size('seq')), 'seq', 0, 0)]
where the time goes in v1:
time: 281 us; the launch traced here: 280 us
  waiting for transfers between devices  116 us (41%)
  local copies, waits for them, and re-layouts  37.8 us (13%)
  blocking collectives  37.7 us (13%)
  matrix products  30.6 us (11%)
  other arithmetic  20.2 us (7%)
  between operations  13.7 us (5%)
  starting transfers between devices  13.1 us (5%)
  loops' own time  10.6 us (4%)
    reduce_scatter x1, waiting for transfers between devices, local(): lax.psum_scatter(jnp.dot(attended, w_out, preferred_element_type=jnp.floa...  67.4 us
    all_to_all x1, blocking collectives, local(): lax.all_to_all(outgoing, ('seq', 'head'), split_axis=0, concat_axis=0, ti...  37.7 us
    all_to_all x1, waiting for transfers between devices, local(): lax.all_to_all(jnp.dot(hidden, w_down[0], preferred_element_type=jnp.floa...  29.7 us
    all_to_all x1, waiting for transfers between devices, local(): lax.all_to_all(jnp.stack([stacked] * lax.axis_size('seq')), 'seq', 0, 0)  19.2 us
    another operation x1, loops' own time, local(): state = lax.fori_loop(0, count // step, inner, initial)  10.4 us
    dot_general x1, matrix products, local(): jnp.dot(hidden, w_down[0], preferred_element_type=jnp.float32)  8.26 us
    all_to_all x1, starting transfers between devices, local(): lax.all_to_all(jnp.stack([stacked] * lax.axis_size('seq')), 'seq', 0, 0)  7.16 us
    all_to_all x1, starting transfers between devices, local(): lax.all_to_all(jnp.dot(hidden, w_down[0], preferred_element_type=jnp.floa...  5.91 us
  transfers between devices with their start and end apart: 3, of which 3 were waited for; matrix products, arithmetic and copies ran while one was open for 5% of the time, Pallas kernels for 0%

profile of v1, /device:TPU:0, one launch (start us, length us, event | category | flops | bytes accessed | tf_op | source)
XLA Modules:
  0.0 280.0 jit_solution(12020925077879993320)
XLA Ops:
  17.4 7.2 %all-to-all-start = ((bf16[16,2,256,128]{3,2,1,0:T(8,128)(2,1)}), bf16[16,2,256,128]{3,2,1,0:T(8,128)(2,1)}, u32[]{:S(2)}, u32[]{:S(2)}) async-start(bf16[16,2,256,128]{3,2,1,0:T(8,128)(2,1)} %stack.8), calls=%async_computation | async-start | bytes 4194304 | tf_op jit(solution)/shard_map/all_to_all | solution.py:129
  25.9 3.5 %fusion.51 = f32[256,512]{1,0:T(8,128)} fusion(bf16[2048,512]{1,0:T(8,128)(2,1)} %param.21, f32[2048]{0:T(1024)} %param.20, f32[256]{0:T(256)S(1)} %add_rsqrt_fusion.2, bf16[256,2048]{1,0:T(8,128)(2,1)} %param.19), kind=kOutput, calls=%fused_computation.99 | convolution fusion | flops 538968064 | bytes 3679232 | tf_op jit(solution)/shard_map/dot_general | solution.py:71
  34.6 19.2 %all-to-all-done = bf16[16,2,256,128]{3,2,1,0:T(8,128)(2,1)} async-done(((bf16[16,2,256,128]{3,2,1,0:T(8,128)(2,1)}), bf16[16,2,256,128]{3,2,1,0:T(8,128)(2,1)}, u32[]{:S(2)}, u32[]{:S(2)}) %all-to-all-start) | async-done | bytes 2097184 | tf_op jit(solution)/shard_map/all_to_all | solution.py:129
  53.9 3.2 %copy.83 = bf16[16,2,256,128]{3,2,0,1:T(8,128)(2,1)} copy(bf16[16,2,256,128]{3,2,1,0:T(8,128)(2,1)} %all-to-all-done) | data formatting | bytes 4194304 | tf_op jit(solution)/shard_map/all_to_all | solution.py:129
  57.9 19.0 %while.22 = (s32[]{:T(128)}, f32[4,256]{1,0:T(4,128)S(1)}, f32[4,256]{1,0:T(4,128)S(1)}, f32[256,4,128]{2,0,1:T(8,128)}, s32[]{:T(128)}, /*index=5*/s32[]{:T(128...) while((s32[]{:T(128)}, f32[4,256]{1,0:T(4,128)S(1)}, ...), condition=%wide.region_12.13_spmd.clone, body=%wide.region_6.12_spmd.clone.sunk | while | flops 276050688 | bytes 16863676 | solution.py:138
  59.2 8.5 %conditional.3 = ((f32[4,256]{1,0:T(4,128)S(1)}, f32[4,256]{1,0:T(4,128)S(1)}, f32[256,4,128]{2,0,1:T(8,128)})) conditional(s32[]{:T(128)} %convert_element_type.143, (f32[4,256]{1,0:T(4,128)S(1)}, f32[4,256]{1,0:T(4,128)S(1)}, f32[256,4,128]{2,0,1:T(8,128)}) %tuple.78, (s32[]{:T(128)}, s32[512]{0:T(512)S(1)}, s32[6]{0:T(128)}, s32[256]{0:T(256)}, ...), branch_computations={%region_7.7_spmd, %region_8.11_spmd} | conditional | flops 276050688 | bytes 16860310 | solution.py:121
  60.9 2.7 fusion.2
  63.6 3.5 %fusion.5 = f32[256,4,128]{2,0,1:T(8,128)} fusion(f32[512,256,4]{1,0,2:T(8,128)} %get-tuple-element.537, f32[4,256]{1,0:T(4,128)S(1)} %get-tuple-element.624, pred[256,512]{0,1:T(8,128)(4,1)S(1)} %and_and_fusion, f32[256,4,128]{2,0,1:T(8,128)} %get-tuple-element.459, f32[256,4]{0,1:T(4,128)S(1)} %get-tuple-element.532, ...), kind=kOutput, calls=%fused_computation.9 | convolution fusion | flops 137101312 | bytes 3416072 | tf_op jit(solution)/shard_map/while/body/eval_jaxpr/cond/branch_1_fun/hqk,kd->qhd/dot_general | solution.py:112
  76.9 2.0 copy.88
  80.0 3.3 %convolution_convert_fusion = bf16[256,2048]{1,0:T(8,128)(2,1)} fusion(bf16[256,512]{0,1:T(8,128)(2,1)S(1)} %bitcast.93, bf16[512,2048]{1,0:T(8,128)(2,1)} %param.26), kind=kOutput, calls=%fused_computation.37 | convolution fusion | flops 537395200 | bytes 3407872 | tf_op jit(solution)/shard_map/dot_general | solution.py:147
  83.4 2.8 %convert_element_type.85 = f32[256,2048]{1,0:T(8,128)} convert(bf16[256,2048]{1,0:T(8,128)(2,1)} %param.19) | non-fusion elementwise | flops 524288 | bytes 3145728 | tf_op jit(solution)/shard_map/convert_element_type | solution.py:69
  87.3 67.4 %reduce-scatter.2.cloned.1.call-done = bf16[32,2048]{1,0:T(8,128)(2,1)} async-done(((bf16[256,2048]{1,0:T(8,128)(2,1)}), bf16[32,2048]{1,0:T(8,128)(2,1)}) %reduce-scatter.2.cloned.1.call-update) | async-done | bytes 131088 | tf_op jit(solution)/shard_map/reduce_scatter | solution.py:146
  157.0 3.7 %scatter_custom_fusion = bf16[512,2048]{1,0:T(8,128)(2,1)} fusion(s32[256]{0:T(256)S(1)} %bitcast.99, bf16[]{:T(256)} %constant.154.clone.1, bf16[32,2048]{1,0:T(8,128)(2,1)S(1)} %multiply_convert_fusion.2), kind=kCustom, calls=%fused_computation.45 | custom fusion | bytes 2228226 | tf_op jit(solution)/shard_map/scatter | solution.py:163
  160.7 4.1 %reshape.318 = bf16[128,4,2048]{2,1,0:T(4,128)(2,1)} reshape(bf16[512,2048]{1,0:T(8,128)(2,1)} %scatter_custom_fusion) | data formatting | bytes 4194304 | tf_op jit(solution)/shard_map/reshape | solution.py:165
  164.8 37.7 %all_to_all.15 = bf16[128,4,2048]{2,1,0:T(4,128)(2,1)} all-to-all(bf16[128,4,2048]{2,1,0:T(4,128)(2,1)} %reshape.318), channel_id=1, replica_groups=mesh['seq'=16,'head'=8] {'seq','head'}, dimensions={0} | all-to-all | bytes 4194304 | tf_op jit(solution)/shard_map/all_to_all | solution.py:166
  202.5 4.0 %reshape.319 = bf16[512,2048]{1,0:T(8,128)(2,1)} reshape(bf16[128,4,2048]{2,1,0:T(4,128)(2,1)} %all_to_all.15) | data formatting | bytes 4194304 | tf_op jit(solution)/shard_map/reshape | solution.py:167
  206.4 5.5 %fusion.22 = f32[512,768]{1,0:T(8,128)} fusion(bf16[512,2048]{1,0:T(8,128)(2,1)} %reshape.319, bf16[1,2048,768]{2,1,0:T(8,128)(2,1)} %param.31), kind=kOutput, calls=%fused_computation.34 | convolution fusion | flops 1610612736 | bytes 6815744 | tf_op jit(solution)/shard_map/dot_general | solution.py:168
  211.9 8.3 %fusion.24 = bf16[512,2048]{1,0:T(8,128)(2,1)} fusion(bf16[1,768,2048]{2,1,0:T(8,128)(2,1)S(1)} %copy-done, f32[512,768]{1,0:T(8,128)} %fusion.22, bf16[512,2048]{1,0:T(8,128)(2,1)} %reshape.319, bf16[1,2048,768]{2,1,0:T(8,128)(2,1)} %param.32), kind=kOutput, calls=%fused_computation.36 | convolution fusion | flops 3224633344 | bytes 12058624 | tf_op jit(solution)/shard_map/dot_general | solution.py:172
  220.2 4.1 %reshape.320 = bf16[128,4,2048]{2,1,0:T(4,128)(2,1)} reshape(bf16[512,2048]{1,0:T(8,128)(2,1)} %fusion.24) | data formatting | bytes 4194304 | tf_op jit(solution)/shard_map/reshape | solution.py:174
  224.3 5.9 %all-to-all-start.2 = ((bf16[128,4,2048]{2,1,0:T(4,128)(2,1)}), bf16[128,4,2048]{2,1,0:T(4,128)(2,1)}, u32[]{:S(2)}, u32[]{:S(2)}) async-start(bf16[128,4,2048]{2,1,0:T(4,128)(2,1)} %reshape.320), calls=%async_computation.3 | async-start | bytes 4194304 | tf_op jit(solution)/shard_map/all_to_all | solution.py:171
  230.3 29.7 %all-to-all-done.2 = bf16[128,4,2048]{2,1,0:T(4,128)(2,1)} async-done(((bf16[128,4,2048]{2,1,0:T(4,128)(2,1)}), bf16[128,4,2048]{2,1,0:T(4,128)(2,1)}, u32[]{:S(2)}, u32[]{:S(2)}) %all-to-all-start.2) | async-done | bytes 2097184 | tf_op jit(solution)/shard_map/all_to_all | solution.py:171
  260.0 4.0 %reshape.321 = bf16[512,2048]{1,0:T(8,128)(2,1)} reshape(bf16[128,4,2048]{2,1,0:T(4,128)(2,1)} %all-to-all-done.2) | data formatting | bytes 4194304 | tf_op jit(solution)/shard_map/reshape | solution.py:180
  264.0 5.2 %gather_fusion = bf16[256,2048]{1,0:T(8,128)(2,1)} fusion(bf16[512,2048]{1,0:T(8,128)(2,1)} %reshape.321, s32[1024]{0:T(1024)S(1)} %pad_clamp_fusion), kind=kCustom, calls=%fused_computation | custom fusion | bytes 2098176 | tf_op jit(solution)/shard_map/gather | solution.py:180
  269.2 2.2 fusion.27
  (109 shorter events, 26.6 us)
Async XLA Ops:
  6.5 205.4 %copy-start = (bf16[1,768,2048]{2,1,0:T(8,128)(2,1)S(1)}, bf16[1,768,2048]{2,1,0:T(8,128)(2,1)}, u32[]{:S(2)}) copy-start(bf16[1,768,2048]{2,1,0:T(8,128)(2,1)} %param.33) | copy-start | bytes 9437188
  6.5 6.5 %copy-start.9 = (f32[2048]{0:T(1024)S(1)}, f32[2048]{0:T(1024)}, u32[]{:S(2)}) copy-start(f32[2048]{0:T(1024)} %param.20) | copy-start | bytes 24580
  6.5 3.7 %copy-start.10 = (s32[6]{0:T(128)S(1)}, s32[6]{0:T(128)}, u32[]{:S(2)}) copy-start(s32[6]{0:T(128)} %param.28) | copy-start | bytes 76
  8.2 6.7 %copy-start.7 = (f32[128]{0:T(128)S(1)}, f32[128]{0:T(128)}, u32[]{:S(2)}) copy-start(f32[128]{0:T(128)} %param.25) | copy-start | bytes 1540
  12.4 0.6 copy-start.3
  17.4 36.5 %all-to-all-start = ((bf16[16,2,256,128]{3,2,1,0:T(8,128)(2,1)}), bf16[16,2,256,128]{3,2,1,0:T(8,128)(2,1)}, u32[]{:S(2)}, u32[]{:S(2)}) async-start(bf16[16,2,256,128]{3,2,1,0:T(8,128)(2,1)} %stack.8), calls=%async_computation | async-start | bytes 4194304 | tf_op jit(solution)/shard_map/all_to_all | solution.py:129
  24.5 130.1 %reduce-scatter.2.cloned.1.call-start = ((), (), s32[]{:S(2)}) async-start(), calls=%async_computation.4 | async-start | bytes 1179648 | tf_op jit(solution)/shard_map/reduce_scatter | solution.py:146
  25.9 7.0 %copy-start.8 = (f32[128]{0:T(128)S(1)}, f32[128]{0:T(128)}, u32[]{:S(2)}) copy-start(f32[128]{0:T(128)} %param.24) | copy-start | bytes 1540
  63.6 3.5 %copy-start.1 = (f32[512,256,4]{1,0,2:T(8,128)S(1)}, f32[512,256,4]{1,0,2:T(8,128)}, u32[]{:S(2)}) copy-start(f32[512,256,4]{1,0,2:T(8,128)} %get-tuple-element.537) | copy-start | bytes 6291460 | tf_op jit(solution)/shard_map/while/body/eval_jaxpr/cond
  83.3 2.9 %copy-start.4 = (s32[32,8]{0,1:T(8,128)S(1)}, s32[32,8]{0,1:T(8,128)}, u32[]{:S(2)}) copy-start(s32[32,8]{0,1:T(8,128)} %param.29) | copy-start | bytes 3076
  83.4 72.4 %copy-start.5 = (f32[2048]{0:T(1024)S(1)}, f32[2048]{0:T(1024)}, u32[]{:S(2)}) copy-start(f32[2048]{0:T(1024)} %param.27) | copy-start | bytes 24580
  224.3 5.9 %copy-start.6 = (f32[32,8]{0,1:T(8,128)S(1)}, f32[32,8]{0,1:T(8,128)}, u32[]{:S(2)}) copy-start(f32[32,8]{0,1:T(8,128)} %param.30) | copy-start | bytes 3076
  224.3 35.7 %all-to-all-start.2 = ((bf16[128,4,2048]{2,1,0:T(4,128)(2,1)}), bf16[128,4,2048]{2,1,0:T(4,128)(2,1)}, u32[]{:S(2)}, u32[]{:S(2)}) async-start(bf16[128,4,2048]{2,1,0:T(4,128)(2,1)} %reshape.320), calls=%async_computation.3 | async-start | bytes 4194304 | tf_op jit(solution)/shard_map/all_to_all | solution.py:171
  264.0 7.5 %copy-start.2 = (bf16[32,2048]{1,0:T(8,128)(2,1)S(1)}, bf16[32,2048]{1,0:T(8,128)(2,1)}, u32[]{:S(2)}) copy-start(bf16[32,2048]{1,0:T(8,128)(2,1)} %reduce-scatter.2.cloned.1.call-done) | copy-start | bytes 393220
Sparse Core Ops, SparseCore 0:
  83.5 71.1 reduce-scatter.1
